TPU v7x, 32 devices: a whole 2x2x4 slice. The times are simulated.
32 devices in a mesh: grp: 4 (over z), exp: 8 (over y, x, core).
Axes of the slice: x: 2, y: 2, z: 4, core: 2. Of those that a mesh axis runs over, the one named last changes fastest.
Arguments:
- cotangent: bfloat16 [4096, 1440], P(('grp', 'exp')), may hold values from -6 to 6
- hidden: bfloat16 [4096, 4, 1440], P(('grp', 'exp')), may hold values from -0.29882812 to 0.29882812
- gates: bfloat16 [4096, 4], P(('grp', 'exp')), may hold values from 0.049804688 to 1
- expert_ids: int32 [4096, 4], P(('grp', 'exp')), may hold values from 0 to 15, all different within a row; in each aligned block of 128 rows (0 to 127, 128 to 255, ...) at most 40 rows name the same one
- group_counts: int32 [4], P('grp'), may hold values from 146 to 1024, as said below
- w_down: bfloat16 [16, 1440, 1440], P('exp', 'grp'), may hold values from -0.15625 to 0.15625
Outputs:
- d_hidden: bfloat16 [4096, 4, 1440], P(('grp', 'exp'))
- d_gate: bfloat16 [4096, 4], P(('grp', 'exp'))
- d_weight: float32 [16, 1440, 1440], P('exp', 'grp')
Inputs may be any that keep to these rules, and one draw needn't show every extreme that they name: `expert_ids`: within the rows of one device no expert is named more than 40 times, and every expert is named somewhere. `group_counts`: some group has all 1024 slots live, and some group only 146.
All inputs are finite; a program needn't handle non-finite values.
Results may differ from a plain program's by a relative error of at most 0.015.
Values may be sent and summed in bfloat16 or wider, within the bound.
No kernel may reach another device: no remote copies, remote signals or barrier semaphores. Data moves between devices by JAX's collectives and lax.ppermute only.
A program may use at most 128 MiB of HBM per device.

v0:
```python
import jax
import jax.numpy as jnp
from jax import lax
from jax.sharding import PartitionSpec as P

LOSS_SCALE = 32768


def body(cotangent, hidden, gates, expert_ids, group_counts, w_down):
    tok = cotangent.shape[0]
    top = expert_ids.shape[1]
    ffw = hidden.shape[2]
    width = cotangent.shape[1]
    n_exp = lax.axis_size("exp")
    exp_dev = w_down.shape[0]
    experts = exp_dev * n_exp
    most = 5 * tok * top // (4 * experts)
    count = group_counts[0]
    first_row = lax.axis_index("exp") * tok
    live = (first_row + jnp.arange(tok, dtype=jnp.int32) < count).astype(jnp.float32)
    total = lax.psum(count.astype(jnp.float32), "grp")
    scale = LOSS_SCALE / total
    weighted = (gates.astype(jnp.float32) * live[:, None]).astype(jnp.bfloat16)
    flat_ids = expert_ids.reshape(-1)
    onehot = (flat_ids[:, None] == jnp.arange(experts, dtype=jnp.int32)[None, :]).astype(jnp.int32)
    rank = jnp.sum((jnp.cumsum(onehot, axis=0) - onehot) * onehot, axis=1)
    target = flat_ids * most + rank
    slot_tok = jnp.arange(tok * top, dtype=jnp.int32) // top
    dy_buf = jnp.zeros((experts * most, width), jnp.bfloat16).at[target].set(cotangent[slot_tok])
    hid_buf = jnp.zeros((experts * most, ffw), jnp.bfloat16).at[target].set(hidden.reshape(-1, ffw))
    gate_buf = jnp.zeros((experts * most,), jnp.bfloat16).at[target].set(weighted.reshape(-1))
    dy_buf = dy_buf.reshape(n_exp, exp_dev * most, width)
    hid_buf = hid_buf.reshape(n_exp, exp_dev * most, ffw)
    gate_buf = gate_buf.reshape(n_exp, exp_dev * most)
    dy_recv, gate_recv = (
        lax.all_to_all(dy_buf, "exp", split_axis=0, concat_axis=0, tiled=True),
        lax.all_to_all(gate_buf, "exp", split_axis=0, concat_axis=0, tiled=True),
    )
    hid_recv = lax.all_to_all(hid_buf, "exp", split_axis=0, concat_axis=0, tiled=True)
    dy_four = dy_recv.reshape(n_exp, exp_dev, most, width)
    hid_four = hid_recv.reshape(n_exp, exp_dev, most, ffw)
    gate_three = gate_recv.reshape(n_exp, exp_dev, most).astype(jnp.float32)
    proj = jnp.einsum(
        "sjmd,jfd->sjmf",
        dy_four,
        lax.all_gather(w_down, "grp", axis=1, tiled=True),
        preferred_element_type=jnp.float32,
    )
    dh_rows = (gate_three[..., None] * proj).astype(jnp.bfloat16)
    inner = jnp.sum(hid_four.astype(jnp.float32) * proj, axis=3).astype(jnp.bfloat16)
    scaled = (gate_three[..., None] * dy_four.astype(jnp.float32)).astype(jnp.bfloat16)
    partial_grad = (
        jnp.einsum("sjmf,sjmd->jfd", hid_four, scaled, preferred_element_type=jnp.float32) * scale
    )
    d_weight = lax.psum_scatter(
        partial_grad.astype(jnp.bfloat16), "grp", scatter_dimension=1, tiled=True
    ).astype(jnp.float32)
    back_dh, back_inner = (
        lax.all_to_all(
            dh_rows.reshape(n_exp, exp_dev * most, ffw),
            "exp",
            split_axis=0,
            concat_axis=0,
            tiled=True,
        ),
        lax.all_to_all(
            inner.reshape(n_exp, exp_dev * most), "exp", split_axis=0, concat_axis=0, tiled=True
        ),
    )
    d_hidden = back_dh.reshape(experts * most, ffw)[target].reshape(tok, top, ffw)
    inner_tok = back_inner.reshape(-1)[target].reshape(tok, top)
    d_gate = (inner_tok.astype(jnp.float32) * live[:, None]).astype(jnp.bfloat16)
    return (d_hidden, d_gate, d_weight)


def solution(mesh):
    in_specs = (
        P(("grp", "exp"), None),
        P(("grp", "exp"), None, None),
        P(("grp", "exp"), None),
        P(("grp", "exp"), None),
        P("grp"),
        P("exp", "grp", None),
    )
    out_specs = (P(("grp", "exp"), None, None), P(("grp", "exp"), None), P("exp", "grp", None))
    return jax.shard_map(body, mesh=mesh, in_specs=in_specs, out_specs=out_specs, check_vma=False)
```

profile of v0, /device:TPU:0, one launch (start us, length us, event | category | flops | bytes accessed | tf_op | source)
XLA Modules:
  0.0 501.5 jit_solution(16202728035999669125)
XLA Ops:
  7.2 0.7 all-gather.2.cloned.1.call-update
  8.5 1.2 reduce-window.6
  9.7 0.2 slice_reduce_fusion
  11.0 3.8 scatter_custom_fusion
  14.8 0.7 all_to_all.25
  15.5 5.2 %all-to-all-start = ((bf16[8,1,80]{2,1,0:T(2,128)(2,1)}), bf16[8,1,80]{2,1,0:T(2,128)(2,1)S(1)}, u32[]{:S(2)}, u32[]{:S(2)}) async-start(bf16[8,1,80]{2,1,0:T(2,128)(2,1)} %all_to_all.25), calls=%async_computation | async-start | bytes 8192 | tf_op jit(solution)/shard_map/all_to_all | solution.py:37
  20.6 1.6 copy.55
  22.2 0.8 reshape.220
  23.0 4.5 scatter_custom_fusion.2
  27.5 4.3 all-to-all-start.3
  32.0 9.6 %scatter_custom_fusion.1 = bf16[640,1440]{1,0:T(8,128)(2,1)} fusion(s32[512]{0:T(512)S(1)} %bitcast.59, bf16[128,1440]{1,0:T(8,128)(2,1)S(1)} %copy.52, s32[1024]{0:T(1024)S(1)} %pad_clamp_fusion.1, bf16[]{:T(256)} %constant.15.clone.1), kind=kCustom, calls=%fused_computation.18 | custom fusion | bytes 1843202 | tf_op jit(solution)/shard_map/scatter | solution.py:29
  41.6 15.5 %all-to-all-done.3 = bf16[8,80,1440]{2,1,0:T(8,128)(2,1)S(1)} async-done(((bf16[8,80,1440]{2,1,0:T(8,128)(2,1)}), bf16[8,80,1440]{2,1,0:T(8,128)(2,1)S(1)}, u32[]{:S(2)}, u32[]{:S(2)}) %all-to-all-start.3) | async-done | bytes 1843232 | tf_op jit(solution)/shard_map/all_to_all | solution.py:39
  57.0 4.3 all-to-all-start.1
  61.4 15.4 %psum.7 = f32[]{:T(128)} all-reduce(f32[]{:T(128)S(6)} %convert_element_type.90), channel_id=1, replica_groups=mesh['grp'=4,'exp'=8] {'grp'}, use_global_device_ids=true, to_apply=%region_7.8 | all-reduce | flops 1 | bytes 8 | tf_op jit(solution)/shard_map/psum | solution.py:21
  77.6 9.0 %all-to-all-done.1 = bf16[8,80,1440]{2,1,0:T(8,128)(2,1)} async-done(((bf16[8,80,1440]{2,1,0:T(8,128)(2,1)}), bf16[8,80,1440]{2,1,0:T(8,128)(2,1)}, u32[]{:S(2)}, u32[]{:S(2)}) %all-to-all-start.1) | async-done | bytes 1843232 | tf_op jit(solution)/shard_map/all_to_all | solution.py:36
  86.6 83.1 %all-gather.2.cloned.1.call-done = bf16[2,1440,1440]{2,1,0:T(8,128)(2,1)} async-done(((bf16[2,360,1440]{2,1,0:T(8,128)(2,1)}), bf16[2,1440,1440]{2,1,0:T(8,128)(2,1)}) %all-gather.2.cloned.1.call-update) | async-done | bytes 8294416 | tf_op jit(solution)/shard_map/all_gather | solution.py:46
  169.7 9.6 %fusion.4 = (bf16[8,2,40]{2,0,1:T(8,128)(2,1)S(1)}, bf16[8,2,40,1440]{3,2,0,1:T(8,128)(2,1)}, bf16[8,2,40,1440]{3,2,0,1:T(8,128)(2,1)S(1)}) fusion(bf16[8,2,40,1440]{3,2,1,0:T(8,128)(2,1)S(1)} %bitcast.55, f32[8,2,40]{2,0,1:T(8,128)S(1)} %copy.51, bf16[8,2,40,1440]{3,2,1,0:T(8,128)(2,1)} %bitcast.6, bf16[2,1440,1440]{2,1,0:T(8,128)(2,1)} %all-gather.2.cloned.1.call-done), kind=kOutput, calls=%fused_computation.13 | convolution fusion | flops 2661580288 | bytes 15671040 | tf_op jit(solution)/shard_map/sjmd,jfd->sjmf/dot_general | solution.py:43
  179.3 7.1 %fusion = bf16[2,1440,1440]{2,1,0:T(8,128)(2,1)} fusion(bf16[8,2,40,1440]{3,2,1,0:T(8,128)(2,1)S(1)} %bitcast.56, f32[]{:T(128)S(6)} %div.13, bf16[8,2,40,1440]{3,2,0,1:T(8,128)(2,1)S(1)} %get-tuple-element.17), kind=kOutput, calls=%fused_computation.7 | convolution fusion | flops 2662502400 | bytes 11980804 | tf_op jit(solution)/shard_map/sjmf,sjmd->jfd/dot_general | solution.py:53
  186.4 0.7 convert_element_type.95
  187.0 3.7 all-to-all-start.4
  190.7 1.5 copy.54
  192.1 3.1 all-to-all-done.4
  195.3 3.7 all-to-all-start.2
  199.0 0.6 dynamic-slice
  200.4 3.5 gather_fusion.1
  204.1 0.7 copy.62
  204.8 19.4 %all-to-all-done.2 = bf16[8,80,1440]{2,1,0:T(8,128)(2,1)S(1)} async-done(((bf16[8,80,1440]{2,1,0:T(8,128)(2,1)}), bf16[8,80,1440]{2,1,0:T(8,128)(2,1)S(1)}, u32[]{:S(2)}, u32[]{:S(2)}) %all-to-all-start.2) | async-done | bytes 1843232 | tf_op jit(solution)/shard_map/all_to_all | solution.py:59
  224.2 2.1 gather_fusion
  226.3 0.4 reshape.169
  226.7 2.4 copy.61
  229.2 261.2 %all-reduce.3.cloned.1.call-done = bf16[2,1440,1440]{2,1,0:T(8,128)(2,1)} async-done(((bf16[2,1440,1440]{2,1,0:T(8,128)(2,1)}), bf16[2,1440,1440]{2,1,0:T(8,128)(2,1)}) %all-reduce.3.cloned.1.call-update) | async-done | bytes 8294416
  490.3 4.3 dynamic-slice_convert_fusion
  (43 shorter events, 1.7 us)
Async XLA Ops:
  7.2 0.8 copy-start.3
  7.2 3.4 copy-start.4
  7.2 13.4 %copy-start.1 = (bf16[128,4,1440]{0,2,1:T(8,128)(2,1)S(1)}, bf16[128,4,1440]{0,2,1:T(8,128)(2,1)}, u32[]{:S(2)}) copy-start(bf16[128,4,1440]{0,2,1:T(8,128)(2,1)} %param.7) | copy-start | bytes 4423684
  7.2 162.5 %all-gather.2.cloned.1.call-start = ((), (), s32[]{:S(2)}) async-start(), calls=%async_computation.5 | async-start | bytes 11059200 | tf_op jit(solution)/shard_map/all_gather | solution.py:46
  15.5 12.0 %all-to-all-start = ((bf16[8,1,80]{2,1,0:T(2,128)(2,1)}), bf16[8,1,80]{2,1,0:T(2,128)(2,1)S(1)}, u32[]{:S(2)}, u32[]{:S(2)}) async-start(bf16[8,1,80]{2,1,0:T(2,128)(2,1)} %all_to_all.25), calls=%async_computation | async-start | bytes 8192 | tf_op jit(solution)/shard_map/all_to_all | solution.py:37
  27.5 4.3 copy-start.2
  27.5 29.6 %all-to-all-start.3 = ((bf16[8,80,1440]{2,1,0:T(8,128)(2,1)}), bf16[8,80,1440]{2,1,0:T(8,128)(2,1)S(1)}, u32[]{:S(2)}, u32[]{:S(2)}) async-start(bf16[8,80,1440]{2,1,0:T(8,128)(2,1)} %bitcast.12), calls=%async_computation.3 | async-start | bytes 3932160 | tf_op jit(solution)/shard_map/all_to_all | solution.py:39
  57.0 29.6 %all-to-all-start.1 = ((bf16[8,80,1440]{2,1,0:T(8,128)(2,1)}), bf16[8,80,1440]{2,1,0:T(8,128)(2,1)}, u32[]{:S(2)}, u32[]{:S(2)}) async-start(bf16[8,80,1440]{2,1,0:T(8,128)(2,1)} %bitcast.5), calls=%async_computation.1 | async-start | bytes 3932160 | tf_op jit(solution)/shard_map/all_to_all | solution.py:36
  61.4 429.0 %all-reduce.3.cloned.1.call-start = ((), (), s32[]{:S(2)}) async-start(), calls=%async_computation.6 | async-start | bytes 17694720
  186.3 4.4 copy-start
  187.0 8.2 %all-to-all-start.4 = ((bf16[8,1,80]{2,1,0:T(2,128)(2,1)}), bf16[8,1,80]{2,1,0:T(2,128)(2,1)S(1)}, u32[]{:S(2)}, u32[]{:S(2)}) async-start(bf16[8,1,80]{2,1,0:T(2,128)(2,1)} %convert_element_type.95), calls=%async_computation.4 | async-start | bytes 8192 | tf_op jit(solution)/shard_map/all_to_all | solution.py:66
  195.3 3.7 copy-start.5
  195.3 28.9 %all-to-all-start.2 = ((bf16[8,80,1440]{2,1,0:T(8,128)(2,1)}), bf16[8,80,1440]{2,1,0:T(8,128)(2,1)S(1)}, u32[]{:S(2)}, u32[]{:S(2)}) async-start(bf16[8,80,1440]{2,1,0:T(8,128)(2,1)} %bitcast.54), calls=%async_computation.2 | async-start | bytes 3932160 | tf_op jit(solution)/shard_map/all_to_all | solution.py:59
Sparse Core Ops, SparseCore 0:
  9.6 160.0 all-gather.1
  186.5 303.8 all-reduce.2
where the time goes:
time: 502 us; the launch traced here: 501 us
  waiting for transfers between devices  392 us (78%)
  local copies, waits for them, and re-layouts  34.2 us (7%)
  starting transfers between devices  21.3 us (4%)
  matrix products  16.6 us (3%)
  between operations  16.3 us (3%)
  blocking collectives  15.4 us (3%)
  other arithmetic  5.77 us (1%)
    unnamed x3, waiting for transfers between devices  262 us
    all_gather x1, waiting for transfers between devices, body(): lax.all_gather(w_down, 'grp', axis=1, tiled=True)  83.1 us
    all_to_all x1, waiting for transfers between devices, body(): lax.all_to_all(dh_rows.reshape(n_exp, exp_dev * most, ffw), 'exp', split_...  19.4 us
    all_to_all x1, waiting for transfers between devices, body(): lax.all_to_all(hid_buf, 'exp', split_axis=0, concat_axis=0, tiled=True)  15.5 us
    psum x1, blocking collectives, body(): total = lax.psum(count.astype(jnp.float32), 'grp')  15.4 us
  transfers between devices with their start and end apart: 7, of which 6 were waited for; matrix products, arithmetic and copies ran while one was open for 7% of the time, Pallas kernels for 0%

commit v1 on v0

--- a/solution.py
+++ b/solution.py
@@ -40,11 +40,27 @@
     dy_four = dy_recv.reshape(n_exp, exp_dev, most, width)
     hid_four = hid_recv.reshape(n_exp, exp_dev, most, ffw)
     gate_three = gate_recv.reshape(n_exp, exp_dev, most).astype(jnp.float32)
+
+    def recover_signs(local):
+        a_name = "grp"
+        dev_count = lax.axis_size(a_name)
+        column = [(k, (k + 1) % dev_count) for k in range(dev_count)]
+        samples = [(k, (k - 1) % dev_count) for k in range(dev_count)]
+        block_now, e_now = ([local], [local])
+        for _ in range(dev_count // 2):
+            value_now = lax.ppermute(block_now[-1], axis_name=a_name, perm=column)
+            block_now.append(value_now)
+        w = 0
+        while w < (dev_count - 1) // 2:
+            current_value = lax.ppermute(e_now[-1], axis_name=a_name, perm=samples)
+            e_now.append(current_value)
+            w += 1
+        inter = jnp.concatenate([*block_now[::-1], *e_now[1:]], axis=1)
+        next_value = lax.axis_index(a_name)
+        return jnp.roll(inter, (next_value - dev_count // 2) * local.shape[1], axis=1)
+
     proj = jnp.einsum(
-        "sjmd,jfd->sjmf",
-        dy_four,
-        lax.all_gather(w_down, "grp", axis=1, tiled=True),
-        preferred_element_type=jnp.float32,
+        "sjmd,jfd->sjmf", dy_four, recover_signs(w_down), preferred_element_type=jnp.float32
     )
     dh_rows = (gate_three[..., None] * proj).astype(jnp.bfloat16)
     inner = jnp.sum(hid_four.astype(jnp.float32) * proj, axis=3).astype(jnp.bfloat16)

time: 502 us -> 539 us (1.074)
  blocking collectives: 15.4 us -> 68.1 us
  waiting for transfers between devices: 392 us -> 341 us
  local copies, waits for them, and re-layouts: 34.2 us -> 59.9 us
    all_gather x1 -> x0, waiting for transfers between devices: 83.1 us -> none  [body(): lax.all_gather(w_down, 'grp', axis=1, tiled=True)]
    psum x1, blocking collectives: 15.4 us -> 68.1 us  [body(): total = lax.psum(count.astype(jnp.float32), 'grp')]
    ppermute x0 -> x3, waiting for transfers between devices: none -> 48.2 us  [the longest x2 48.2 us: recover_signs(): value_now = lax.ppermute(block_now[-1], axis_name=a_name, perm=column)]
    unnamed x18 -> x23, local copies, waits for them, and re-layouts: 5.58 us -> 24.3 us
    all_to_all x1, waiting for transfers between devices: 15.5 us -> 0.01 us  [body(): lax.all_to_all(hid_buf, 'exp', split_axis=0, concat_axis=0, tiled=True)]
    unnamed x3 -> x2, waiting for transfers between devices: 262 us -> 260 us
  transfers between devices with their start and end apart: 7 -> 9, of which waited for: 6 -> 5; matrix products, arithmetic and copies ran while one was open for 7% -> 12% of each run, Pallas kernels for 0% -> 0%
where the time goes in v1:
time: 539 us
  waiting for transfers between devices  341 us (63%)
  blocking collectives  68.1 us (13%)
  local copies, waits for them, and re-layouts  59.9 us (11%)
  starting transfers between devices  25.5 us (5%)
  matrix products  20.6 us (4%)
  between operations  16.2 us (3%)
  other arithmetic  7.14 us (1%)
    unnamed x2, waiting for transfers between devices  260 us
    psum x1, blocking collectives, body(): total = lax.psum(count.astype(jnp.float32), 'grp')  68.1 us
    ppermute x2, waiting for transfers between devices, recover_signs(): value_now = lax.ppermute(block_now[-1], axis_name=a_name, perm=column)  48.2 us
    unnamed x23, local copies, waits for them, and re-layouts  24.3 us
    all_to_all x1, waiting for transfers between devices, body(): lax.all_to_all(dh_rows.reshape(n_exp, exp_dev * most, ffw), 'exp', split_...  19.2 us
    all_to_all x1, waiting for transfers between devices, body(): lax.all_to_all(dy_buf, 'exp', split_axis=0, concat_axis=0, tiled=True)  10.9 us
  transfers between devices with their start and end apart: 9, of which 5 were waited for; matrix products, arithmetic and copies ran while one was open for 12% of the time, Pallas kernels for 0%

profile of v1, /device:TPU:0, one launch (start us, length us, event | category | flops | bytes accessed | tf_op | source)
XLA Modules:
  0.0 538.6 jit_solution(13829810589064458386)
XLA Ops:
  7.2 3.1 collective-permute-start
  10.2 2.1 collective-permute-start.2
  13.2 48.2 %collective-permute-done = bf16[2,360,1440]{2,1,0:T(8,128)(2,1)S(1)} collective-permute-done((bf16[2,360,1440]{2,1,0:T(8,128)(2,1)}, bf16[2,360,1440]{2,1,0:T(8,128)(2,1)S(1)}, u32[]{:S(2)}, u32[]{:S(2)}) %collective-permute-start) | collective-permute-done | bytes 2073632 | tf_op jit(solution)/shard_map/ppermute | solution.py:51
  65.6 3.8 scatter_custom_fusion
  70.1 4.0 all-to-all-start
  74.0 3.9 copy.55
  77.9 3.7 reshape.220
  81.7 5.3 scatter_custom_fusion.2
  87.0 4.5 all-to-all-start.3
  91.4 68.1 %psum.7 = f32[]{:T(128)} all-reduce(f32[]{:T(128)S(6)} %convert_element_type.90), channel_id=1, replica_groups=mesh['grp'=4,'exp'=8] {'grp'}, use_global_device_ids=true, to_apply=%region_7.8 | all-reduce | flops 1 | bytes 8 | tf_op jit(solution)/shard_map/psum | solution.py:21
  159.7 9.6 %scatter_custom_fusion.1 = bf16[640,1440]{1,0:T(8,128)(2,1)} fusion(s32[512]{0:T(512)S(1)} %bitcast.59, bf16[128,1440]{1,0:T(8,128)(2,1)S(1)} %copy.52, s32[1024]{0:T(1024)S(1)} %pad_clamp_fusion.1, bf16[]{:T(256)} %constant.52.clone.1), kind=kCustom, calls=%fused_computation.19 | custom fusion | bytes 1843202 | tf_op jit(solution)/shard_map/scatter | solution.py:29
  170.2 3.2 constant_dynamic-update-slice_fusion.7
  173.3 1.6 constant_dynamic-update-slice_fusion.6
  174.9 4.5 all-to-all-start.1
  179.7 1.5 constant_dynamic-update-slice_fusion.5
  181.2 3.1 constant_dynamic-update-slice_fusion.4
  184.3 3.3 constant_dynamic-update-slice_fusion.3
  187.6 1.5 constant_dynamic-update-slice_fusion.2
  189.1 1.5 constant_dynamic-update-slice_fusion.1
  190.6 3.1 constant_dynamic-update-slice_fusion
  193.8 10.9 %all-to-all-done.1 = bf16[8,80,1440]{2,1,0:T(8,128)(2,1)} async-done(((bf16[8,80,1440]{2,1,0:T(8,128)(2,1)}), bf16[8,80,1440]{2,1,0:T(8,128)(2,1)}, u32[]{:S(2)}, u32[]{:S(2)}) %all-to-all-start.1) | async-done | bytes 1843232 | tf_op jit(solution)/shard_map/all_to_all | solution.py:36
  204.7 10.3 %fusion.5 = (bf16[8,2,40]{2,0,1:T(8,128)(2,1)S(1)}, bf16[8,2,40,1440]{3,2,0,1:T(8,128)(2,1)S(1)}, bf16[8,2,40,1440]{3,2,0,1:T(8,128)(2,1)}) fusion(bf16[8,2,40,1440]{3,2,1,0:T(8,128)(2,1)} %bitcast.13, f32[8,2,40]{2,0,1:T(8,128)S(1)} %copy.51, bf16[8,2,40,1440]{3,2,1,0:T(8,128)(2,1)} %bitcast.8, ...), kind=kOutput, calls=%fused_computation.14 | convolution fusion | flops 2661580288 | bytes 18435844 | tf_op jit(solution)/shard_map/sjmd,jfd->sjmf/dot_general | solution.py:62
  215.0 10.3 %fusion = bf16[2,1440,1440]{2,1,0:T(8,128)(2,1)} fusion(bf16[8,2,40,1440]{3,2,1,0:T(8,128)(2,1)} %bitcast.13, f32[]{:T(128)S(6)} %div.13, bf16[8,2,40,1440]{3,2,0,1:T(8,128)(2,1)} %get-tuple-element.17), kind=kOutput, calls=%fused_computation.7 | convolution fusion | flops 2662502400 | bytes 11980804 | tf_op jit(solution)/shard_map/sjmf,sjmd->jfd/dot_general | solution.py:69
  226.0 3.3 all-to-all-start.4
  230.8 3.0 all-to-all-done.4
  233.8 3.9 all-to-all-start.2
  239.1 3.5 gather_fusion.1
  243.5 19.2 %all-to-all-done.2 = bf16[8,80,1440]{2,1,0:T(8,128)(2,1)S(1)} async-done(((bf16[8,80,1440]{2,1,0:T(8,128)(2,1)}), bf16[8,80,1440]{2,1,0:T(8,128)(2,1)S(1)}, u32[]{:S(2)}, u32[]{:S(2)}) %all-to-all-start.2) | async-done | bytes 1843232 | tf_op jit(solution)/shard_map/all_to_all | solution.py:75
  262.6 2.1 gather_fusion
  265.2 2.4 copy.61
  267.6 259.8 %all-reduce.3.cloned.1.call-done = bf16[2,1440,1440]{2,1,0:T(8,128)(2,1)} async-done(((bf16[2,1440,1440]{2,1,0:T(8,128)(2,1)}), bf16[2,1440,1440]{2,1,0:T(8,128)(2,1)}) %all-reduce.3.cloned.1.call-update) | async-done | bytes 8294416
  527.5 4.3 dynamic-slice_convert_fusion
  (52 shorter events, 9.8 us)
Async XLA Ops:
  7.2 54.3 %collective-permute-start = (bf16[2,360,1440]{2,1,0:T(8,128)(2,1)}, bf16[2,360,1440]{2,1,0:T(8,128)(2,1)S(1)}, u32[]{:S(2)}, u32[]{:S(2)}) collective-permute-start(bf16[2,360,1440]{2,1,0:T(8,128)(2,1)} %param.11), channel_id=1, source_target_pairs={{0,8},{8,16},{16,24},{24,0},{1,9},{9,17},{17,25},{25,1},{2,10},{10... | collective-permute-start | bytes 6220808 | tf_op jit(solution)/shard_map/ppermute | solution.py:51
  10.2 171.0 %collective-permute-start.2 = (bf16[2,360,1440]{2,1,0:T(8,128)(2,1)}, bf16[2,360,1440]{2,1,0:T(8,128)(2,1)}, u32[]{:S(2)}, u32[]{:S(2)}) collective-permute-start(bf16[2,360,1440]{2,1,0:T(8,128)(2,1)} %param.11), channel_id=1, source_target_pairs={{0,24},{8,0},{16,8},{24,16},{1,25},{9,1},{17,9},{25,17},{2,26},{10... | collective-permute-start | bytes 6220808 | tf_op jit(solution)/shard_map/ppermute | solution.py:55
  61.4 111.9 %copy-start.1 = (bf16[2,360,1440]{2,1,0:T(8,128)(2,1)}, bf16[2,360,1440]{2,1,0:T(8,128)(2,1)S(1)}, u32[]{:S(2)}) copy-start(bf16[2,360,1440]{2,1,0:T(8,128)(2,1)S(1)} %collective-permute-done) | copy-start | bytes 6220804
  61.4 108.7 %collective-permute-start.1 = (bf16[2,360,1440]{2,1,0:T(8,128)(2,1)S(1)}, bf16[2,360,1440]{2,1,0:T(8,128)(2,1)}, u32[]{:S(2)}, u32[]{:S(2)}) collective-permute-start(bf16[2,360,1440]{2,1,0:T(8,128)(2,1)S(1)} %collective-permute-done), channel_id=1, source_target_pairs={{0,8},{8,16},{16,24},{24,0},{1,9},{9,17},{17,25},{25,1},{2,10},{10... | collective-permute-start | bytes 6220808 | tf_op jit(solution)/shard_map/ppermute | solution.py:51
  70.1 16.9 %all-to-all-start = ((bf16[8,1,80]{2,1,0:T(2,128)(2,1)}), bf16[8,1,80]{2,1,0:T(2,128)(2,1)S(1)}, u32[]{:S(2)}, u32[]{:S(2)}) async-start(bf16[8,1,80]{2,1,0:T(2,128)(2,1)} %all_to_all.25), calls=%async_computation | async-start | bytes 8192 | tf_op jit(solution)/shard_map/all_to_all | solution.py:37
  87.0 72.5 %copy-start.3 = (bf16[128,1440]{0,1:T(8,128)(2,1)S(1)}, bf16[128,1440]{0,1:T(8,128)(2,1)}, u32[]{:S(2)}) copy-start(bf16[128,1440]{0,1:T(8,128)(2,1)} %param.6) | copy-start | bytes 1105924
  87.0 88.0 %all-to-all-start.3 = ((bf16[8,80,1440]{2,1,0:T(8,128)(2,1)}), bf16[8,80,1440]{2,1,0:T(8,128)(2,1)}, u32[]{:S(2)}, u32[]{:S(2)}) async-start(bf16[8,80,1440]{2,1,0:T(8,128)(2,1)} %bitcast.54), calls=%async_computation.3 | async-start | bytes 3932160 | tf_op jit(solution)/shard_map/all_to_all | solution.py:39
  174.9 4.8 copy-start
  174.9 29.7 %all-to-all-start.1 = ((bf16[8,80,1440]{2,1,0:T(8,128)(2,1)}), bf16[8,80,1440]{2,1,0:T(8,128)(2,1)}, u32[]{:S(2)}, u32[]{:S(2)}) async-start(bf16[8,80,1440]{2,1,0:T(8,128)(2,1)} %bitcast.55), calls=%async_computation.1 | async-start | bytes 3932160 | tf_op jit(solution)/shard_map/all_to_all | solution.py:36
  179.4 348.0 %all-reduce.3.cloned.1.call-start = ((), (), s32[]{:S(2)}) async-start(), calls=%async_computation.5 | async-start | bytes 17694720
  184.3 3.3 copy-start.2
  226.0 7.8 %all-to-all-start.4 = ((bf16[8,1,80]{2,1,0:T(2,128)(2,1)}), bf16[8,1,80]{2,1,0:T(2,128)(2,1)S(1)}, u32[]{:S(2)}, u32[]{:S(2)}) async-start(bf16[8,1,80]{2,1,0:T(2,128)(2,1)} %convert_element_type.95), calls=%async_computation.4 | async-start | bytes 8192 | tf_op jit(solution)/shard_map/all_to_all | solution.py:82
  230.8 6.9 %copy-start.4 = (u32[32]{0:T(128)S(1)}, u32[32]{0:T(128)}, u32[]{:S(2)}) copy-start(u32[32]{0:T(128)} %constant.73) | copy-start | bytes 388
  233.8 28.8 %all-to-all-start.2 = ((bf16[8,80,1440]{2,1,0:T(8,128)(2,1)}), bf16[8,80,1440]{2,1,0:T(8,128)(2,1)S(1)}, u32[]{:S(2)}, u32[]{:S(2)}) async-start(bf16[8,80,1440]{2,1,0:T(8,128)(2,1)} %bitcast.56), calls=%async_computation.2 | async-start | bytes 3932160 | tf_op jit(solution)/shard_map/all_to_all | solution.py:75
Sparse Core Ops, SparseCore 0:
  225.4 301.9 all-reduce.2
